TPU v7x, 256 devices: a whole 4x4x8 slice. The times are simulated.
256 devices in a mesh: tm: 32 (over y, z_hi, core), rows: 8 (over z_lo, x).
Axes of the slice: x: 4, y: 4, z: 8 (z_hi: 4, z_lo: 2; z = z_hi * 2 + z_lo), core: 2. Of those that a mesh axis runs over, the one named last changes fastest.
Arguments:
- latent: bfloat16 [32, 16, 128, 512], P('tm', 'rows'), may hold values from -32 to 32
- norm_gain: float32 [512], replicated, may hold values from 0.1 to 1.9
- conv_weight: bfloat16 [27, 512, 512], P(None, 'tm'), may hold values from -0.0546875 to 0.0546875
- grad_out: bfloat16 [32, 16, 128, 512], P('tm', 'rows'), may hold values from -6 to 6
Outputs:
- refined: bfloat16 [32, 16, 128, 512], P('tm', 'rows')
- grad_latent: float32 [32, 16, 128, 512], P('tm', 'rows')
All inputs are finite; a program needn't handle non-finite values.
Results may differ from a plain program's by a relative error of at most 0.0013.
The roundings to bfloat16 on the way count: a program that leaves them out, or rounds other values in their place, can miss the bound.
Values may be sent and summed in bfloat16 or wider, within the bound.
No kernel may reach another device: no remote copies, remote signals or barrier semaphores. Data moves between devices by JAX's collectives and lax.ppermute only.
A program may use at most 64 MiB of HBM per device.

v0:
```python
import jax
import jax.numpy as jnp
from jax import lax
from jax.sharding import PartitionSpec as P

GROUPS = 32
epsilon = 1e-06


def shifted(block, axis, distance):
    devices = range(lax.axis_size(axis))
    route = [(i - distance, i) for i in devices if i - distance in devices]
    return lax.ppermute(block, axis, route)


def with_halo(shard, sides, width):
    for axis, dim in sides:
        size, length = (lax.axis_size(axis), shard.shape[dim])
        up = [(i, (i + 1) % size) for i in range(size - 1)]
        down = [(j, i) for i, j in up]
        last = lax.slice_in_dim(shard, length - width, length, axis=dim)
        first = lax.slice_in_dim(shard, 0, width, axis=dim)
        before = lax.ppermute(last, axis, up)
        after = lax.ppermute(first, axis, down)
        shard = jnp.concatenate([before, shard, after], axis=dim)
    return shard


def grouped_view(values):
    return values.reshape(
        values.shape[0], values.shape[1] * values.shape[2], GROUPS, values.shape[3] // GROUPS
    )


def widen_columns(values):
    return jnp.pad(values, ((0, 0), (0, 0), (1, 1), (0, 0)))


def shards(latent, norm_gain, conv_weight, grad_out):
    frames_here, rows_here, columns, channels = latent.shape
    cell_count = lax.axis_size("rows") * rows_here * columns * (channels // GROUPS)
    full_weight = lax.all_gather(conv_weight, "tm", axis=1, tiled=True)
    latent_wide = latent.astype(jnp.float32)
    grouped = grouped_view(latent_wide)
    average = lax.psum(jnp.sum(grouped, axis=(1, 3)), "rows") / cell_count
    centred = grouped - average[:, None, :, None]
    spread = lax.psum(jnp.sum(centred * centred, axis=(1, 3)), "rows") / cell_count
    inverse = lax.rsqrt(spread + epsilon)
    normed_grouped = centred * inverse[:, None, :, None]
    normed = normed_grouped.reshape(latent.shape)
    scaled = normed * norm_gain
    sigmoid_value = jax.nn.sigmoid(scaled)
    activated = (scaled * sigmoid_value).astype(jnp.bfloat16)
    before_one = shifted(activated, "tm", 1)
    before_two = shifted(activated, "tm", 2)
    padded = with_halo(
        jnp.concatenate([before_two, before_one, activated], axis=0), (("rows", 1),), 1
    )
    after_one = shifted(grad_out, "tm", -1)
    after_two = shifted(grad_out, "tm", -2)
    padded_grad = with_halo(
        jnp.concatenate([grad_out, after_one, after_two], axis=0), (("rows", 1),), 1
    )
    padded = widen_columns(padded)
    padded_grad = widen_columns(padded_grad)
    conv_sum = jnp.zeros((frames_here * rows_here * columns, channels), jnp.float32)
    grad_act = jnp.zeros((frames_here * rows_here * columns, channels), jnp.float32)
    for time_tap in range(3):
        for row_tap in range(3):
            for col_tap in range(3):
                tap_weight = full_weight[time_tap * 9 + row_tap * 3 + col_tap]
                window = padded[
                    time_tap : time_tap + frames_here,
                    row_tap : row_tap + rows_here,
                    col_tap : col_tap + columns,
                ]
                conv_sum = conv_sum + jnp.dot(
                    window.reshape(-1, channels), tap_weight, preferred_element_type=jnp.float32
                )
                back_window = padded_grad[
                    2 - time_tap : 2 - time_tap + frames_here,
                    2 - row_tap : 2 - row_tap + rows_here,
                    2 - col_tap : 2 - col_tap + columns,
                ]
                grad_act = grad_act + lax.dot_general(
                    back_window.reshape(-1, channels),
                    tap_weight,
                    (((1,), (1,)), ((), ())),
                    preferred_element_type=jnp.float32,
                )
    refined = (latent_wide + conv_sum.reshape(latent.shape)).astype(jnp.bfloat16)
    grad_scaled = (
        grad_act.reshape(latent.shape) * sigmoid_value * (1.0 + scaled * (1.0 - sigmoid_value))
    )
    grad_normed = grouped_view(grad_scaled * norm_gain)
    first_sum, second_sum = lax.psum(
        (jnp.sum(grad_normed, axis=(1, 3)), jnp.sum(grad_normed * normed_grouped, axis=(1, 3))),
        "rows",
    )
    first = first_sum / cell_count
    second = second_sum / cell_count
    grad_norm_part = (
        grad_normed - first[:, None, :, None] - normed_grouped * second[:, None, :, None]
    ) * inverse[:, None, :, None]
    grad_latent = grad_out.astype(jnp.float32) + grad_norm_part.reshape(latent.shape)
    return (refined, grad_latent)


def solution(mesh):
    placed = (P("tm", "rows", None, None), P(), P(None, "tm", None), P("tm", "rows", None, None))
    return jax.shard_map(
        shards,
        mesh=mesh,
        in_specs=placed,
        out_specs=(P("tm", "rows", None, None), P("tm", "rows", None, None)),
        check_vma=False,
    )
```

profile of v0, /device:TPU:6, one launch (start us, length us, event | category | flops | bytes accessed | tf_op | source)
XLA Modules:
  0.0 219.8 jit_solution(12708673439425601817)
XLA Ops:
  7.2 0.7 all-gather.2.cloned.1.call-update
  7.9 1.3 collective-permute-start.4
  9.2 1.3 collective-permute-start.5
  10.5 1.0 convert_reduce_fusion
  11.7 16.1 %psum.28 = f32[1,32]{1,0:T(1,128)S(1)} all-reduce(f32[1,32]{1,0:T(1,128)S(1)} %bitcast.290), channel_id=1, replica_groups=mesh['tm'=32,'rows'=8] {'rows'}, use_global_device_ids=true, to_apply=%region_2.0 | all-reduce | flops 32 | bytes 256 | tf_op jit(solution)/shard_map/psum | solution.py:45
  27.8 1.0 constant_dynamic-update-slice_fusion.2
  28.8 5.3 %collective-permute-done.5 = bf16[1,2,128,512]{3,2,1,0:T(8,128)(2,1)S(1)} collective-permute-done((bf16[1,2,128,512]{3,2,1,0:T(8,128)(2,1)}, bf16[1,2,128,512]{3,2,1,0:T(8,128)(2,1)S(1)}, u32[]{:S(2)}, u32[]{:S(2)}) %collective-permute-start.5) | collective-permute-done | bytes 262176 | tf_op jit(solution)/shard_map/ppermute | solution.py:13
  34.3 0.6 copy-done.7
  34.9 1.9 collective-permute-start.6
  36.8 3.9 %collective-permute-start.7 = (bf16[3,1,128,512]{3,2,1,0:T(8,128)(2,1)S(1)}, bf16[3,1,128,512]{3,2,1,0:T(8,128)(2,1)S(1)}, u32[]{:S(2)}, u32[]{:S(2)}) collective-permute-start(bf16[3,1,128,512]{3,2,1,0:T(8,128)(2,1)S(1)} %get-tuple-element.59), channel_id=1, source_target_pairs={{1,0},{2,1},{3,2},{4,3},{5,4},{6,5},{7,6},{9,8},{10,9},{11,10},{12... | collective-permute-start | bytes 1179656 | tf_op jit(solution)/shard_map/ppermute | solution.py:24
  40.9 1.0 fusion.31
  42.1 22.3 %psum.29 = f32[1,32]{1,0:T(1,128)S(1)} all-reduce(f32[1,32]{1,0:T(1,128)S(1)} %bitcast.291), channel_id=1, replica_groups=mesh['tm'=32,'rows'=8] {'rows'}, use_global_device_ids=true, to_apply=%region_5.6 | all-reduce | flops 32 | bytes 256 | tf_op jit(solution)/shard_map/psum | solution.py:47
  64.6 1.2 pad_maximum_fusion.6
  65.8 0.4 select_maximum_fusion
  66.2 1.7 fusion.87
  67.9 52.9 %all-gather.2.cloned.1.call-done = bf16[27,512,512]{2,1,0:T(8,128)(2,1)} async-done(((bf16[27,16,512]{2,1,0:T(8,128)(2,1)}), bf16[27,512,512]{2,1,0:T(8,128)(2,1)}) %all-gather.2.cloned.1.call-update) | async-done | bytes 14155792 | tf_op jit(solution)/shard_map/all_gather | solution.py:42
  120.8 1.6 fusion.59
  122.4 2.1 fusion.41
  124.6 2.2 fusion.77
  126.7 1.4 fusion.53
  128.2 1.5 fusion.35
  129.7 1.5 fusion.71
  131.1 1.5 fusion.81
  132.6 1.4 fusion.65
  134.0 1.4 fusion.47
  135.5 1.5 fusion.79
  137.0 1.5 fusion.33
  138.4 1.3 fusion.75
  141.1 0.3 fusion.61
  144.5 0.8 fusion.8
  145.3 0.3 fusion.85
  145.7 2.3 %collective-permute-start.1 = (bf16[1,2,128,512]{3,2,1,0:T(8,128)(2,1)S(1)}, bf16[1,2,128,512]{3,2,1,0:T(8,128)(2,1)S(1)}, u32[]{:S(2)}, u32[]{:S(2)}) collective-permute-start(bf16[1,2,128,512]{3,2,1,0:T(8,128)(2,1)S(1)} %get-tuple-element.62), channel_id=1, source_target_pairs={{0,8},{8,16},{16,24},{24,32},{32,40},{40,48},{48,56},{56,64},{64,7... | collective-permute-start | bytes 786440 | tf_op jit(solution)/shard_map/ppermute | solution.py:13
  148.0 6.9 %collective-permute-start = (bf16[1,2,128,512]{3,2,1,0:T(8,128)(2,1)S(1)}, bf16[1,2,128,512]{3,2,1,0:T(8,128)(2,1)S(1)}, u32[]{:S(2)}, u32[]{:S(2)}) collective-permute-start(bf16[1,2,128,512]{3,2,1,0:T(8,128)(2,1)S(1)} %get-tuple-element.62), channel_id=1, source_target_pairs={{0,16},{8,24},{16,32},{24,40},{32,48},{40,56},{48,64},{56,72},{64,... | collective-permute-start | bytes 786440 | tf_op jit(solution)/shard_map/ppermute | solution.py:13
  155.2 22.7 %all-reduce.2 = (f32[1,32]{1,0:T(1,128)S(1)}, f32[1,32]{1,0:T(1,128)S(1)}) all-reduce(f32[1,32]{1,0:T(1,128)S(1)} %bitcast.289, f32[1,32]{1,0:T(1,128)S(1)} %bitcast.288), channel_id=1, replica_groups=mesh['tm'=32,'rows'=8] {'rows'}, use_global_device_ids=true, to_apply=%region_11.12 | all-reduce | flops 64 | bytes 512 | tf_op jit(solution)/shard_map/psum | solution.py:96
  178.3 1.3 fusion.78
  179.8 3.7 %collective-permute-start.2 = (bf16[3,1,128,512]{3,2,1,0:T(8,128)(2,1)S(1)}, bf16[3,1,128,512]{3,2,1,0:T(8,128)(2,1)S(1)}, u32[]{:S(2)}, u32[]{:S(2)}) collective-permute-start(bf16[3,1,128,512]{3,2,1,0:T(8,128)(2,1)S(1)} %get-tuple-element.60), channel_id=1, source_target_pairs={{0,1},{1,2},{2,3},{3,4},{4,5},{5,6},{6,7},{8,9},{9,10},{10,11},{11... | collective-permute-start | bytes 1179656 | tf_op jit(solution)/shard_map/ppermute | solution.py:23
  183.6 2.3 %collective-permute-start.3 = (bf16[3,1,128,512]{3,2,1,0:T(8,128)(2,1)S(1)}, bf16[3,1,128,512]{3,2,1,0:T(8,128)(2,1)S(1)}, u32[]{:S(2)}, u32[]{:S(2)}) collective-permute-start(bf16[3,1,128,512]{3,2,1,0:T(8,128)(2,1)S(1)} %get-tuple-element.61), channel_id=1, source_target_pairs={{1,0},{2,1},{3,2},{4,3},{5,4},{6,5},{7,6},{9,8},{10,9},{11,10},{12... | collective-permute-start | bytes 1179656 | tf_op jit(solution)/shard_map/ppermute | solution.py:24
  185.9 1.5 fusion.42
  187.4 1.3 fusion.60
  188.7 4.1 %collective-permute-done.2 = bf16[3,1,128,512]{3,2,1,0:T(8,128)(2,1)S(1)} collective-permute-done((bf16[3,1,128,512]{3,2,1,0:T(8,128)(2,1)S(1)}, bf16[3,1,128,512]{3,2,1,0:T(8,128)(2,1)S(1)}, u32[]{:S(2)}, u32[]{:S(2)}) %collective-permute-start.2) | collective-permute-done | bytes 393248 | tf_op jit(solution)/shard_map/ppermute | solution.py:23
  192.9 5.6 %collective-permute-done.3 = bf16[3,1,128,512]{3,2,1,0:T(8,128)(2,1)S(1)} collective-permute-done((bf16[3,1,128,512]{3,2,1,0:T(8,128)(2,1)S(1)}, bf16[3,1,128,512]{3,2,1,0:T(8,128)(2,1)S(1)}, u32[]{:S(2)}, u32[]{:S(2)}) %collective-permute-start.3) | collective-permute-done | bytes 393248 | tf_op jit(solution)/shard_map/ppermute | solution.py:24
  198.4 0.7 select_maximum_fusion.2
  199.2 0.8 fusion.88
  200.1 1.8 fusion.66
  202.0 1.3 fusion.48
  203.3 1.3 fusion.82
  210.8 1.1 fusion.11
  211.9 1.1 fusion.30
  (91 shorter events, 12.2 us)
Async XLA Ops:
  7.2 117.4 %copy-start.2 = (bf16[1,2,128,512]{3,2,1,0:T(8,128)(2,1)S(1)}, bf16[1,2,128,512]{3,2,1,0:T(8,128)(2,1)}, u32[]{:S(2)}) copy-start(bf16[1,2,128,512]{3,2,1,0:T(8,128)(2,1)} %param.7) | copy-start | bytes 786436
  7.2 113.7 %all-gather.2.cloned.1.call-start = ((), (), s32[]{:S(2)}) async-start(), calls=%async_computation | async-start | bytes 14598144 | tf_op jit(solution)/shard_map/all_gather | solution.py:42
  7.9 20.9 %collective-permute-start.4 = (bf16[1,2,128,512]{3,2,1,0:T(8,128)(2,1)}, bf16[1,2,128,512]{3,2,1,0:T(8,128)(2,1)S(1)}, u32[]{:S(2)}, u32[]{:S(2)}) collective-permute-start(bf16[1,2,128,512]{3,2,1,0:T(8,128)(2,1)} %param.7), channel_id=1, source_target_pairs={{8,0},{16,8},{24,16},{32,24},{40,32},{48,40},{56,48},{64,56},{72,6... | collective-permute-start | bytes 786440 | tf_op jit(solution)/shard_map/ppermute | solution.py:13
  9.2 24.9 %collective-permute-start.5 = (bf16[1,2,128,512]{3,2,1,0:T(8,128)(2,1)}, bf16[1,2,128,512]{3,2,1,0:T(8,128)(2,1)S(1)}, u32[]{:S(2)}, u32[]{:S(2)}) collective-permute-start(bf16[1,2,128,512]{3,2,1,0:T(8,128)(2,1)} %param.7), channel_id=1, source_target_pairs={{16,0},{24,8},{32,16},{40,24},{48,32},{56,40},{64,48},{72,56},{80,... | collective-permute-start | bytes 786440 | tf_op jit(solution)/shard_map/ppermute | solution.py:13
  28.8 5.5 %copy-start.6 = (bf16[1,2,128,512]{3,2,1,0:T(8,128)(2,1)}, bf16[1,2,128,512]{3,2,1,0:T(8,128)(2,1)S(1)}, u32[]{:S(2)}) copy-start(bf16[1,2,128,512]{3,2,1,0:T(8,128)(2,1)S(1)} %collective-permute-done.4) | copy-start | bytes 786436
  34.2 0.7 copy-start.7
  34.9 29.8 %collective-permute-start.6 = (bf16[3,1,128,512]{3,2,1,0:T(8,128)(2,1)S(1)}, bf16[3,1,128,512]{3,2,1,0:T(8,128)(2,1)S(1)}, u32[]{:S(2)}, u32[]{:S(2)}) collective-permute-start(bf16[3,1,128,512]{3,2,1,0:T(8,128)(2,1)S(1)} %get-tuple-element.58), channel_id=1, source_target_pairs={{0,1},{1,2},{2,3},{3,4},{4,5},{5,6},{6,7},{8,9},{9,10},{10,11},{11... | collective-permute-start | bytes 1179656 | tf_op jit(solution)/shard_map/ppermute | solution.py:23
  36.8 27.9 %collective-permute-start.7 = (bf16[3,1,128,512]{3,2,1,0:T(8,128)(2,1)S(1)}, bf16[3,1,128,512]{3,2,1,0:T(8,128)(2,1)S(1)}, u32[]{:S(2)}, u32[]{:S(2)}) collective-permute-start(bf16[3,1,128,512]{3,2,1,0:T(8,128)(2,1)S(1)} %get-tuple-element.59), channel_id=1, source_target_pairs={{1,0},{2,1},{3,2},{4,3},{5,4},{6,5},{7,6},{9,8},{10,9},{11,10},{12... | collective-permute-start | bytes 1179656 | tf_op jit(solution)/shard_map/ppermute | solution.py:24
  120.8 17.6 %copy-start = (bf16[27,512,512]{2,1,0:T(8,128)(2,1)S(1)}, bf16[27,512,512]{2,1,0:T(8,128)(2,1)}, u32[]{:S(2)}) copy-start(bf16[27,512,512]{2,1,0:T(8,128)(2,1)} %all-gather.2.cloned.1.call-done) | copy-start | bytes 42467332
  120.8 18.9 %copy-start.5 = (bf16[1,2,128,512]{3,2,1,0:T(8,128)(2,1)S(1)}, bf16[1,2,128,512]{3,2,1,0:T(8,128)(2,1)}, u32[]{:S(2)}) copy-start(bf16[1,2,128,512]{3,2,1,0:T(8,128)(2,1)} %get-tuple-element.11) | copy-start | bytes 786436
  120.8 19.2 %copy-start.4 = (bf16[1,2,128,512]{3,2,1,0:T(8,128)(2,1)S(1)}, bf16[1,2,128,512]{3,2,1,0:T(8,128)(2,1)}, u32[]{:S(2)}) copy-start(bf16[1,2,128,512]{3,2,1,0:T(8,128)(2,1)} %get-tuple-element.12) | copy-start | bytes 786436
  120.8 19.6 %copy-start.3 = (bf16[1,2,128,512]{3,2,1,0:T(8,128)(2,1)S(1)}, bf16[1,2,128,512]{3,2,1,0:T(8,128)(2,1)}, u32[]{:S(2)}) copy-start(bf16[1,2,128,512]{3,2,1,0:T(8,128)(2,1)} %get-tuple-element.13) | copy-start | bytes 786436
  141.1 4.2 %copy-start.1 = (bf16[1,2,128,512]{3,2,1,0:T(8,128)(2,1)S(1)}, bf16[1,2,128,512]{3,2,1,0:T(8,128)(2,1)}, u32[]{:S(2)}) copy-start(bf16[1,2,128,512]{3,2,1,0:T(8,128)(2,1)} %param.4) | copy-start | bytes 786436
  141.1 4.2 %copy-start.8 = (f32[512]{0:T(512)S(1)}, f32[512]{0:T(512)}, u32[]{:S(2)}) copy-start(f32[512]{0:T(512)} %param.5) | copy-start | bytes 6148
  145.3 59.3 %slice-start = ((s8[14155776]{0:T(1024)(128)(4,1)}), s8[1572864]{0:T(1024)(128)(4,1)S(1)}, s32[]{:S(2)}) async-start(s8[14155776]{0:T(1024)(128)(4,1)} %bitcast.231), calls=%async_computation.1 | async-start | bytes 3145728
  145.7 34.0 %collective-permute-start.1 = (bf16[1,2,128,512]{3,2,1,0:T(8,128)(2,1)S(1)}, bf16[1,2,128,512]{3,2,1,0:T(8,128)(2,1)S(1)}, u32[]{:S(2)}, u32[]{:S(2)}) collective-permute-start(bf16[1,2,128,512]{3,2,1,0:T(8,128)(2,1)S(1)} %get-tuple-element.62), channel_id=1, source_target_pairs={{0,8},{8,16},{16,24},{24,32},{32,40},{40,48},{48,56},{56,64},{64,7... | collective-permute-start | bytes 786440 | tf_op jit(solution)/shard_map/ppermute | solution.py:13
  148.0 31.7 %collective-permute-start = (bf16[1,2,128,512]{3,2,1,0:T(8,128)(2,1)S(1)}, bf16[1,2,128,512]{3,2,1,0:T(8,128)(2,1)S(1)}, u32[]{:S(2)}, u32[]{:S(2)}) collective-permute-start(bf16[1,2,128,512]{3,2,1,0:T(8,128)(2,1)S(1)} %get-tuple-element.62), channel_id=1, source_target_pairs={{0,16},{8,24},{16,32},{24,40},{32,48},{40,56},{48,64},{56,72},{64,... | collective-permute-start | bytes 786440 | tf_op jit(solution)/shard_map/ppermute | solution.py:13
  179.8 13.0 %collective-permute-start.2 = (bf16[3,1,128,512]{3,2,1,0:T(8,128)(2,1)S(1)}, bf16[3,1,128,512]{3,2,1,0:T(8,128)(2,1)S(1)}, u32[]{:S(2)}, u32[]{:S(2)}) collective-permute-start(bf16[3,1,128,512]{3,2,1,0:T(8,128)(2,1)S(1)} %get-tuple-element.60), channel_id=1, source_target_pairs={{0,1},{1,2},{2,3},{3,4},{4,5},{5,6},{6,7},{8,9},{9,10},{10,11},{11... | collective-permute-start | bytes 1179656 | tf_op jit(solution)/shard_map/ppermute | solution.py:23
  183.6 14.8 %collective-permute-start.3 = (bf16[3,1,128,512]{3,2,1,0:T(8,128)(2,1)S(1)}, bf16[3,1,128,512]{3,2,1,0:T(8,128)(2,1)S(1)}, u32[]{:S(2)}, u32[]{:S(2)}) collective-permute-start(bf16[3,1,128,512]{3,2,1,0:T(8,128)(2,1)S(1)} %get-tuple-element.61), channel_id=1, source_target_pairs={{1,0},{2,1},{3,2},{4,3},{5,4},{6,5},{7,6},{9,8},{10,9},{11,10},{12... | collective-permute-start | bytes 1179656 | tf_op jit(solution)/shard_map/ppermute | solution.py:24
  185.9 18.8 %slice-start.1 = ((s8[14155776]{0:T(1024)(128)(4,1)}), s8[4194304]{0:T(1024)(128)(4,1)S(1)}, s32[]{:S(2)}) async-start(s8[14155776]{0:T(1024)(128)(4,1)} %bitcast.231), calls=%async_computation.2 | async-start | bytes 8388608
  199.2 5.5 %slice-start.2 = ((s8[14155776]{0:T(1024)(128)(4,1)}), s8[4194304]{0:T(1024)(128)(4,1)S(1)}, s32[]{:S(2)}) async-start(s8[14155776]{0:T(1024)(128)(4,1)} %bitcast.231), calls=%async_computation.3 | async-start | bytes 8388608
  199.9 4.7 %slice-start.3 = ((s8[14155776]{0:T(1024)(128)(4,1)}), s8[4194304]{0:T(1024)(128)(4,1)S(1)}, s32[]{:S(2)}) async-start(s8[14155776]{0:T(1024)(128)(4,1)} %bitcast.231), calls=%async_computation.4 | async-start | bytes 8388608
Sparse Core Ops, SparseCore 0:
  10.6 110.1 all-gather.1
where the time goes:
time: 221 us; the launch traced here: 220 us
  waiting for transfers between devices  68.6 us (31%)
  blocking collectives  61.2 us (28%)
  matrix products  39.8 us (18%)
  starting transfers between devices  23.6 us (11%)
  between operations  14.8 us (7%)
  other arithmetic  6.57 us (3%)
  local copies, waits for them, and re-layouts  5.16 us (2%)
    all_gather x1, waiting for transfers between devices, shards(): full_weight = lax.all_gather(conv_weight, 'tm', axis=1, tiled=True)  52.9 us
    dot_general x27, matrix products, shards(): lax.dot_general(back_window.reshape(-1, channels), tap_weight, (((1,), (1...  24.2 us
    psum x1, blocking collectives, shards(): lax.psum((jnp.sum(grad_normed, axis=(1, 3)), jnp.sum(grad_normed * normed...  22.7 us
    psum x1, blocking collectives, shards(): lax.psum(jnp.sum(centred * centred, axis=(1, 3)), 'rows') / cell_count  22.3 us
    psum x1, blocking collectives, shards(): average = lax.psum(jnp.sum(grouped, axis=(1, 3)), 'rows') / cell_count  16.1 us
    dot_general x27, matrix products, shards(): jnp.dot(window.reshape(-1, channels), tap_weight, preferred_element_type=...  15.7 us
    ppermute x4, starting transfers between devices, shifted(): return lax.ppermute(block, axis, route)  11.8 us
    ppermute x2, starting transfers between devices, with_halo(): after = lax.ppermute(first, axis, down)  6.21 us
  transfers between devices with their start and end apart: 9, of which 4 were waited for; matrix products, arithmetic and copies ran while one was open for 5% of the time, Pallas kernels for 0%

commit v1 on v0

--- a/solution.py
+++ b/solution.py
@@ -5,6 +5,11 @@
 
 GROUPS = 32
 epsilon = 1e-06
+
+
+def gather_and_add(array, name):
+    pieces = lax.all_gather(array, name)
+    return jnp.sum(pieces, axis=0)
 
 
 def shifted(block, axis, distance):
@@ -42,7 +47,7 @@
     full_weight = lax.all_gather(conv_weight, "tm", axis=1, tiled=True)
     latent_wide = latent.astype(jnp.float32)
     grouped = grouped_view(latent_wide)
-    average = lax.psum(jnp.sum(grouped, axis=(1, 3)), "rows") / cell_count
+    average = gather_and_add(jnp.sum(grouped, axis=(1, 3)), "rows") / cell_count
     centred = grouped - average[:, None, :, None]
     spread = lax.psum(jnp.sum(centred * centred, axis=(1, 3)), "rows") / cell_count
     inverse = lax.rsqrt(spread + epsilon)

time: 221 us -> 220 us (level)
  starting transfers between devices: 23.6 us -> 21.1 us
    unnamed x0 -> x1, blocking collectives: none -> 16.4 us
    psum x1 -> x0, blocking collectives: 16.1 us -> none  [shards(): average = lax.psum(jnp.sum(grouped, axis=(1, 3)), 'rows') / cell_count]
    ppermute x4, starting transfers between devices: 11.8 us -> 8.31 us  [shifted(): return lax.ppermute(block, axis, route)]
    all_gather x1, waiting for transfers between devices: 52.9 us -> 56 us  [shards(): full_weight = lax.all_gather(conv_weight, 'tm', axis=1, tiled=True)]
    ppermute x4, waiting for transfers between devices: 5.33 us -> 2.72 us  [shifted(): return lax.ppermute(block, axis, route)]
  transfers between devices with their start and end apart: 9 -> 9, of which waited for: 4 -> 4; matrix products, arithmetic and copies ran while one was open for 5% -> 6% of each run, Pallas kernels for 0% -> 0%
where the time goes in v1:
time: 220 us; the launch traced here: 219 us
  waiting for transfers between devices  68.5 us (31%)
  blocking collectives  60.8 us (28%)
  matrix products  39.8 us (18%)
  starting transfers between devices  21.1 us (10%)
  between operations  15.5 us (7%)
  local copies, waits for them, and re-layouts  6.74 us (3%)
  other arithmetic  6.58 us (3%)
    all_gather x1, waiting for transfers between devices, shards(): full_weight = lax.all_gather(conv_weight, 'tm', axis=1, tiled=True)  56 us
    dot_general x27, matrix products, shards(): lax.dot_general(back_window.reshape(-1, channels), tap_weight, (((1,), (1...  24.2 us
    psum x1, blocking collectives, shards(): lax.psum(jnp.sum(centred * centred, axis=(1, 3)), 'rows') / cell_count  22.5 us
    psum x1, blocking collectives, shards(): lax.psum((jnp.sum(grad_normed, axis=(1, 3)), jnp.sum(grad_normed * normed...  21.9 us
    unnamed x1, blocking collectives  16.4 us
    dot_general x27, matrix products, shards(): jnp.dot(window.reshape(-1, channels), tap_weight, preferred_element_type=...  15.7 us
    ppermute x4, starting transfers between devices, shifted(): return lax.ppermute(block, axis, route)  8.31 us
    ppermute x2, starting transfers between devices, with_halo(): before = lax.ppermute(last, axis, up)  7.79 us
  transfers between devices with their start and end apart: 9, of which 4 were waited for; matrix products, arithmetic and copies ran while one was open for 6% of the time, Pallas kernels for 0%

profile of v1, /device:TPU:6, one launch (start us, length us, event | category | flops | bytes accessed | tf_op | source)
XLA Modules:
  0.0 219.0 jit_solution(14112690406929366861)
XLA Ops:
  7.2 0.7 all-gather.3.cloned.1.call-update
  7.9 1.3 collective-permute-start.4
  9.2 1.3 collective-permute-start.5
  10.5 1.0 convert_reduce_fusion
  11.6 1.3 dynamic-slice
  13.9 16.4 %all-reduce.2 = f32[256]{0:T(256)S(1)} all-reduce(f32[256]{0:T(256)S(1)} %dynamic-update-slice), channel_id=2, replica_groups=mesh['tm'=32,'rows'=8] {'rows'}, use_global_device_ids=true, to_apply=%add.2 | all-reduce | flops 256 | bytes 2048
  30.4 1.0 constant_dynamic-update-slice_fusion.2
  31.4 2.7 %collective-permute-done.5 = bf16[1,2,128,512]{3,2,1,0:T(8,128)(2,1)S(1)} collective-permute-done((bf16[1,2,128,512]{3,2,1,0:T(8,128)(2,1)}, bf16[1,2,128,512]{3,2,1,0:T(8,128)(2,1)S(1)}, u32[]{:S(2)}, u32[]{:S(2)}) %collective-permute-start.5) | collective-permute-done | bytes 262176 | tf_op jit(solution)/shard_map/ppermute | solution.py:18
  34.3 0.6 copy-done.7
  34.9 4.0 %collective-permute-start.6 = (bf16[3,1,128,512]{3,2,1,0:T(8,128)(2,1)S(1)}, bf16[3,1,128,512]{3,2,1,0:T(8,128)(2,1)S(1)}, u32[]{:S(2)}, u32[]{:S(2)}) collective-permute-start(bf16[3,1,128,512]{3,2,1,0:T(8,128)(2,1)S(1)} %get-tuple-element.58), channel_id=1, source_target_pairs={{0,1},{1,2},{2,3},{3,4},{4,5},{5,6},{6,7},{8,9},{9,10},{10,11},{11... | collective-permute-start | bytes 1179656 | tf_op jit(solution)/shard_map/ppermute | solution.py:28
  38.9 1.9 collective-permute-start.7
  41.0 1.0 fusion.31
  42.2 22.5 %psum.21 = f32[1,32]{1,0:T(1,128)S(1)} all-reduce(f32[1,32]{1,0:T(1,128)S(1)} %bitcast.288), channel_id=1, replica_groups=mesh['tm'=32,'rows'=8] {'rows'}, use_global_device_ids=true, to_apply=%region_5.6 | all-reduce | flops 32 | bytes 256 | tf_op jit(solution)/shard_map/psum | solution.py:52
  64.9 1.2 pad_maximum_fusion.6
  66.1 0.4 select_maximum_fusion
  66.5 1.7 fusion.87
  68.2 56.0 %all-gather.3.cloned.1.call-done = bf16[27,512,512]{2,1,0:T(8,128)(2,1)} async-done(((bf16[27,16,512]{2,1,0:T(8,128)(2,1)}), bf16[27,512,512]{2,1,0:T(8,128)(2,1)}) %all-gather.3.cloned.1.call-update) | async-done | bytes 14155792 | tf_op jit(solution)/shard_map/all_gather | solution.py:47
  124.2 1.6 fusion.59
  125.8 2.1 fusion.41
  127.9 2.2 fusion.77
  130.1 1.5 fusion.53
  131.5 1.4 fusion.35
  133.0 1.4 fusion.71
  134.4 1.4 fusion.81
  135.9 1.4 fusion.65
  137.3 1.4 fusion.47
  138.8 1.5 fusion.79
  140.3 1.5 fusion.33
  141.7 1.3 fusion.75
  147.8 0.8 fusion.8
  148.6 0.3 fusion.85
  149.0 2.3 %collective-permute-start.1 = (bf16[1,2,128,512]{3,2,1,0:T(8,128)(2,1)S(1)}, bf16[1,2,128,512]{3,2,1,0:T(8,128)(2,1)S(1)}, u32[]{:S(2)}, u32[]{:S(2)}) collective-permute-start(bf16[1,2,128,512]{3,2,1,0:T(8,128)(2,1)S(1)} %get-tuple-element.62), channel_id=1, source_target_pairs={{0,8},{8,16},{16,24},{24,32},{32,40},{40,48},{48,56},{56,64},{64,7... | collective-permute-start | bytes 786440 | tf_op jit(solution)/shard_map/ppermute | solution.py:18
  151.3 3.4 %collective-permute-start = (bf16[1,2,128,512]{3,2,1,0:T(8,128)(2,1)S(1)}, bf16[1,2,128,512]{3,2,1,0:T(8,128)(2,1)S(1)}, u32[]{:S(2)}, u32[]{:S(2)}) collective-permute-start(bf16[1,2,128,512]{3,2,1,0:T(8,128)(2,1)S(1)} %get-tuple-element.62), channel_id=1, source_target_pairs={{0,16},{8,24},{16,32},{24,40},{32,48},{40,56},{48,64},{56,72},{64,... | collective-permute-start | bytes 786440 | tf_op jit(solution)/shard_map/ppermute | solution.py:18
  155.1 21.9 %all-reduce.3 = (f32[1,32]{1,0:T(1,128)S(1)}, f32[1,32]{1,0:T(1,128)S(1)}) all-reduce(f32[1,32]{1,0:T(1,128)S(1)} %bitcast.287, f32[1,32]{1,0:T(1,128)S(1)} %bitcast.286), channel_id=1, replica_groups=mesh['tm'=32,'rows'=8] {'rows'}, use_global_device_ids=true, to_apply=%region_11.12 | all-reduce | flops 64 | bytes 512 | tf_op jit(solution)/shard_map/psum | solution.py:101
  177.3 1.3 fusion.78
  178.9 3.8 %collective-permute-start.2 = (bf16[3,1,128,512]{3,2,1,0:T(8,128)(2,1)S(1)}, bf16[3,1,128,512]{3,2,1,0:T(8,128)(2,1)S(1)}, u32[]{:S(2)}, u32[]{:S(2)}) collective-permute-start(bf16[3,1,128,512]{3,2,1,0:T(8,128)(2,1)S(1)} %get-tuple-element.60), channel_id=1, source_target_pairs={{0,1},{1,2},{2,3},{3,4},{4,5},{5,6},{6,7},{8,9},{9,10},{10,11},{11... | collective-permute-start | bytes 1179656 | tf_op jit(solution)/shard_map/ppermute | solution.py:28
  182.6 3.0 %collective-permute-start.3 = (bf16[3,1,128,512]{3,2,1,0:T(8,128)(2,1)S(1)}, bf16[3,1,128,512]{3,2,1,0:T(8,128)(2,1)S(1)}, u32[]{:S(2)}, u32[]{:S(2)}) collective-permute-start(bf16[3,1,128,512]{3,2,1,0:T(8,128)(2,1)S(1)} %get-tuple-element.61), channel_id=1, source_target_pairs={{1,0},{2,1},{3,2},{4,3},{5,4},{6,5},{7,6},{9,8},{10,9},{11,10},{12... | collective-permute-start | bytes 1179656 | tf_op jit(solution)/shard_map/ppermute | solution.py:29
  185.7 1.5 fusion.42
  187.2 1.3 fusion.60
  188.5 3.4 %collective-permute-done.2 = bf16[3,1,128,512]{3,2,1,0:T(8,128)(2,1)S(1)} collective-permute-done((bf16[3,1,128,512]{3,2,1,0:T(8,128)(2,1)S(1)}, bf16[3,1,128,512]{3,2,1,0:T(8,128)(2,1)S(1)}, u32[]{:S(2)}, u32[]{:S(2)}) %collective-permute-start.2) | collective-permute-done | bytes 393248 | tf_op jit(solution)/shard_map/ppermute | solution.py:28
  191.9 5.8 %collective-permute-done.3 = bf16[3,1,128,512]{3,2,1,0:T(8,128)(2,1)S(1)} collective-permute-done((bf16[3,1,128,512]{3,2,1,0:T(8,128)(2,1)S(1)}, bf16[3,1,128,512]{3,2,1,0:T(8,128)(2,1)S(1)}, u32[]{:S(2)}, u32[]{:S(2)}) %collective-permute-start.3) | collective-permute-done | bytes 393248 | tf_op jit(solution)/shard_map/ppermute | solution.py:29
  197.7 0.7 select_maximum_fusion.2
  198.4 0.8 fusion.88
  199.4 1.8 fusion.66
  201.2 1.3 fusion.48
  202.5 1.3 fusion.82
  210.0 1.1 fusion.11
  211.1 1.1 fusion.30
  (96 shorter events, 12.9 us)
Async XLA Ops:
  7.2 120.7 %copy-start.2 = (bf16[1,2,128,512]{3,2,1,0:T(8,128)(2,1)S(1)}, bf16[1,2,128,512]{3,2,1,0:T(8,128)(2,1)}, u32[]{:S(2)}) copy-start(bf16[1,2,128,512]{3,2,1,0:T(8,128)(2,1)} %param.7) | copy-start | bytes 786436
  7.2 117.0 %all-gather.3.cloned.1.call-start = ((), (), s32[]{:S(2)}) async-start(), calls=%async_computation | async-start | bytes 14598144 | tf_op jit(solution)/shard_map/all_gather | solution.py:47
  7.9 23.5 %collective-permute-start.4 = (bf16[1,2,128,512]{3,2,1,0:T(8,128)(2,1)}, bf16[1,2,128,512]{3,2,1,0:T(8,128)(2,1)S(1)}, u32[]{:S(2)}, u32[]{:S(2)}) collective-permute-start(bf16[1,2,128,512]{3,2,1,0:T(8,128)(2,1)} %param.7), channel_id=1, source_target_pairs={{8,0},{16,8},{24,16},{32,24},{40,32},{48,40},{56,48},{64,56},{72,6... | collective-permute-start | bytes 786440 | tf_op jit(solution)/shard_map/ppermute | solution.py:18
  9.2 24.9 %collective-permute-start.5 = (bf16[1,2,128,512]{3,2,1,0:T(8,128)(2,1)}, bf16[1,2,128,512]{3,2,1,0:T(8,128)(2,1)S(1)}, u32[]{:S(2)}, u32[]{:S(2)}) collective-permute-start(bf16[1,2,128,512]{3,2,1,0:T(8,128)(2,1)} %param.7), channel_id=1, source_target_pairs={{16,0},{24,8},{32,16},{40,24},{48,32},{56,40},{64,48},{72,56},{80,... | collective-permute-start | bytes 786440 | tf_op jit(solution)/shard_map/ppermute | solution.py:18
  31.4 2.9 %copy-start.6 = (bf16[1,2,128,512]{3,2,1,0:T(8,128)(2,1)}, bf16[1,2,128,512]{3,2,1,0:T(8,128)(2,1)S(1)}, u32[]{:S(2)}) copy-start(bf16[1,2,128,512]{3,2,1,0:T(8,128)(2,1)S(1)} %collective-permute-done.4) | copy-start | bytes 786436
  34.2 0.7 copy-start.7
  34.9 30.1 %collective-permute-start.6 = (bf16[3,1,128,512]{3,2,1,0:T(8,128)(2,1)S(1)}, bf16[3,1,128,512]{3,2,1,0:T(8,128)(2,1)S(1)}, u32[]{:S(2)}, u32[]{:S(2)}) collective-permute-start(bf16[3,1,128,512]{3,2,1,0:T(8,128)(2,1)S(1)} %get-tuple-element.58), channel_id=1, source_target_pairs={{0,1},{1,2},{2,3},{3,4},{4,5},{5,6},{6,7},{8,9},{9,10},{10,11},{11... | collective-permute-start | bytes 1179656 | tf_op jit(solution)/shard_map/ppermute | solution.py:28
  38.9 26.0 %collective-permute-start.7 = (bf16[3,1,128,512]{3,2,1,0:T(8,128)(2,1)S(1)}, bf16[3,1,128,512]{3,2,1,0:T(8,128)(2,1)S(1)}, u32[]{:S(2)}, u32[]{:S(2)}) collective-permute-start(bf16[3,1,128,512]{3,2,1,0:T(8,128)(2,1)S(1)} %get-tuple-element.59), channel_id=1, source_target_pairs={{1,0},{2,1},{3,2},{4,3},{5,4},{6,5},{7,6},{9,8},{10,9},{11,10},{12... | collective-permute-start | bytes 1179656 | tf_op jit(solution)/shard_map/ppermute | solution.py:29
  124.1 17.6 %copy-start = (bf16[27,512,512]{2,1,0:T(8,128)(2,1)S(1)}, bf16[27,512,512]{2,1,0:T(8,128)(2,1)}, u32[]{:S(2)}) copy-start(bf16[27,512,512]{2,1,0:T(8,128)(2,1)} %all-gather.3.cloned.1.call-done) | copy-start | bytes 42467332
  124.1 18.9 %copy-start.5 = (bf16[1,2,128,512]{3,2,1,0:T(8,128)(2,1)S(1)}, bf16[1,2,128,512]{3,2,1,0:T(8,128)(2,1)}, u32[]{:S(2)}) copy-start(bf16[1,2,128,512]{3,2,1,0:T(8,128)(2,1)} %get-tuple-element.11) | copy-start | bytes 786436
  124.2 19.2 %copy-start.4 = (bf16[1,2,128,512]{3,2,1,0:T(8,128)(2,1)S(1)}, bf16[1,2,128,512]{3,2,1,0:T(8,128)(2,1)}, u32[]{:S(2)}) copy-start(bf16[1,2,128,512]{3,2,1,0:T(8,128)(2,1)} %get-tuple-element.12) | copy-start | bytes 786436
  124.2 19.6 %copy-start.3 = (bf16[1,2,128,512]{3,2,1,0:T(8,128)(2,1)S(1)}, bf16[1,2,128,512]{3,2,1,0:T(8,128)(2,1)}, u32[]{:S(2)}) copy-start(bf16[1,2,128,512]{3,2,1,0:T(8,128)(2,1)} %get-tuple-element.13) | copy-start | bytes 786436
  144.4 4.2 %copy-start.1 = (bf16[1,2,128,512]{3,2,1,0:T(8,128)(2,1)S(1)}, bf16[1,2,128,512]{3,2,1,0:T(8,128)(2,1)}, u32[]{:S(2)}) copy-start(bf16[1,2,128,512]{3,2,1,0:T(8,128)(2,1)} %param.4) | copy-start | bytes 786436
  144.4 4.2 %copy-start.8 = (f32[512]{0:T(512)S(1)}, f32[512]{0:T(512)}, u32[]{:S(2)}) copy-start(f32[512]{0:T(512)} %param.5) | copy-start | bytes 6148
  148.6 55.2 %slice-start = ((s8[14155776]{0:T(1024)(128)(4,1)}), s8[1572864]{0:T(1024)(128)(4,1)S(1)}, s32[]{:S(2)}) async-start(s8[14155776]{0:T(1024)(128)(4,1)} %bitcast.229), calls=%async_computation.1 | async-start | bytes 3145728
  149.0 29.7 %collective-permute-start.1 = (bf16[1,2,128,512]{3,2,1,0:T(8,128)(2,1)S(1)}, bf16[1,2,128,512]{3,2,1,0:T(8,128)(2,1)S(1)}, u32[]{:S(2)}, u32[]{:S(2)}) collective-permute-start(bf16[1,2,128,512]{3,2,1,0:T(8,128)(2,1)S(1)} %get-tuple-element.62), channel_id=1, source_target_pairs={{0,8},{8,16},{16,24},{24,32},{32,40},{40,48},{48,56},{56,64},{64,7... | collective-permute-start | bytes 786440 | tf_op jit(solution)/shard_map/ppermute | solution.py:18
  151.3 27.4 %collective-permute-start = (bf16[1,2,128,512]{3,2,1,0:T(8,128)(2,1)S(1)}, bf16[1,2,128,512]{3,2,1,0:T(8,128)(2,1)S(1)}, u32[]{:S(2)}, u32[]{:S(2)}) collective-permute-start(bf16[1,2,128,512]{3,2,1,0:T(8,128)(2,1)S(1)} %get-tuple-element.62), channel_id=1, source_target_pairs={{0,16},{8,24},{16,32},{24,40},{32,48},{40,56},{48,64},{56,72},{64,... | collective-permute-start | bytes 786440 | tf_op jit(solution)/shard_map/ppermute | solution.py:18
  178.9 13.0 %collective-permute-start.2 = (bf16[3,1,128,512]{3,2,1,0:T(8,128)(2,1)S(1)}, bf16[3,1,128,512]{3,2,1,0:T(8,128)(2,1)S(1)}, u32[]{:S(2)}, u32[]{:S(2)}) collective-permute-start(bf16[3,1,128,512]{3,2,1,0:T(8,128)(2,1)S(1)} %get-tuple-element.60), channel_id=1, source_target_pairs={{0,1},{1,2},{2,3},{3,4},{4,5},{5,6},{6,7},{8,9},{9,10},{10,11},{11... | collective-permute-start | bytes 1179656 | tf_op jit(solution)/shard_map/ppermute | solution.py:28
  182.6 15.0 %collective-permute-start.3 = (bf16[3,1,128,512]{3,2,1,0:T(8,128)(2,1)S(1)}, bf16[3,1,128,512]{3,2,1,0:T(8,128)(2,1)S(1)}, u32[]{:S(2)}, u32[]{:S(2)}) collective-permute-start(bf16[3,1,128,512]{3,2,1,0:T(8,128)(2,1)S(1)} %get-tuple-element.61), channel_id=1, source_target_pairs={{1,0},{2,1},{3,2},{4,3},{5,4},{6,5},{7,6},{9,8},{10,9},{11,10},{12... | collective-permute-start | bytes 1179656 | tf_op jit(solution)/shard_map/ppermute | solution.py:29
  185.7 18.2 %slice-start.1 = ((s8[14155776]{0:T(1024)(128)(4,1)}), s8[4194304]{0:T(1024)(128)(4,1)S(1)}, s32[]{:S(2)}) async-start(s8[14155776]{0:T(1024)(128)(4,1)} %bitcast.229), calls=%async_computation.2 | async-start | bytes 8388608
  198.4 5.5 %slice-start.2 = ((s8[14155776]{0:T(1024)(128)(4,1)}), s8[4194304]{0:T(1024)(128)(4,1)S(1)}, s32[]{:S(2)}) async-start(s8[14155776]{0:T(1024)(128)(4,1)} %bitcast.229), calls=%async_computation.3 | async-start | bytes 8388608
  199.2 4.7 %slice-start.3 = ((s8[14155776]{0:T(1024)(128)(4,1)}), s8[4194304]{0:T(1024)(128)(4,1)S(1)}, s32[]{:S(2)}) async-start(s8[14155776]{0:T(1024)(128)(4,1)} %bitcast.229), calls=%async_computation.4 | async-start | bytes 8388608
Sparse Core Ops, SparseCore 0:
  10.6 113.4 all-gather.2
